TPU v7x, 32 devices: a whole 2x2x4 slice. The times are simulated.
32 devices in a mesh: species: 4 (over z), space: 8 (over y, x, core).
Axes of the slice: x: 2, y: 2, z: 4, core: 2. Of those that a mesh axis runs over, the one named last changes fastest.
Arguments:
- density: float32 [4, 32, 16, 32, 128], P('species', None, 'space'), may hold values from 0 to 2
- space_factor: float32 [16, 32, 128], P('space'), may hold values from 0.5 to 1
- diff_rate: float32 [4, 32], P('species'), may hold values from 0.02 to 0.08
- loss_inverse: float32 [4, 32, 32], P('species'), may hold values from 0 to 1, as said below
- chain_yield: float32 [4, 32], P('species'), may hold values from 0.25 to 0.95
- survival: float32 [4, 32], P('species'), may hold values from 0.6 to 1
- gamma_yield: float32 [4, 32], P('species'), may hold values from 0.1 to 1
- sky_weight: bfloat16 [8, 8, 64, 128], P('space'), may hold values from -0.75 to 0.75
- sky_blocks: int32 [8, 8], P('space'), may hold values from 0 to 383
Outputs:
- propagated: float32 [4, 32, 16, 32, 128], P('species', None, 'space')
- sky: float32 [384, 128], P('space')
Inputs may be any that keep to these rules, and one draw needn't show every extreme that they name: `loss_inverse`: each matrix is upper triangular with a diagonal of 0.5 to 1 and nonnegative entries.
All inputs are finite; a program needn't handle non-finite values.
Results may differ from a plain program's by a relative error of at most 0.0011.
Values sent between devices are 32-bit elements; how exact they have to be, the bound alone decides.
No kernel may reach another device: no remote copies, remote signals or barrier semaphores. Data moves between devices by JAX's collectives and lax.ppermute only.
A program may use at most 64 MiB of HBM per device.

v0:
```python
import jax
import jax.numpy as jnp
from jax import lax
from jax.sharding import PartitionSpec as P

SUBSTEPS = 2
NB = 384


def padded_2(cells, sides, width):
    for axis, dim in sides:
        count = lax.axis_size(axis)
        ends = count - 1
        head = lax.slice_in_dim(cells, 0, width, axis=dim)
        tail = lax.slice_in_dim(cells, cells.shape[dim] - width, cells.shape[dim], axis=dim)
        cells = jnp.concatenate(
            [
                lax.ppermute(tail, axis, [(i, (i + 1) % count) for i in range(ends)]),
                cells,
                lax.ppermute(head, axis, [((i + 1) % count, i) for i in range(ends)]),
            ],
            axis=dim,
        )
    return cells


def from_behind(block, axis, distance):
    devices = range(lax.axis_size(axis))
    route = [(i - distance, i) for i in devices if i - distance in devices]
    return lax.ppermute(block, axis, route)


def cross_sum(field):
    padded = jnp.pad(field, ((0, 0), (0, 0), (1, 1), (1, 1)))
    beside = padded[:, :, 2:, 1:-1] + padded[:, :, :-2, 1:-1]
    beside = beside + padded[:, :, 1:-1, 2:] + padded[:, :, 1:-1, :-2]
    return beside


def body(
    density,
    space_factor,
    diff_rate,
    loss_inverse,
    chain_yield,
    survival,
    gamma_yield,
    sky_weight,
    sky_blocks,
):
    field = density[0]
    bins = field.shape[0]
    width = field.shape[1]
    rate = diff_rate[0][:, None, None, None]
    factor = rate * space_factor[None]
    for step in range(SUBSTEPS):
        wider = padded_2(field, (("space", 1),), 1)
        beside = wider[:, 2:] + wider[:, :-2] + cross_sum(field)
        field = field + factor * (beside - 6.0 * field)
    solved = jnp.dot(
        loss_inverse[0],
        field.reshape(bins, -1),
        precision=lax.Precision.HIGHEST,
        preferred_element_type=jnp.float32,
    ).reshape(field.shape)
    factor_chain = chain_yield[0][:, None, None, None]
    own_part = survival[0][:, None, None, None] * solved
    carried = own_part
    for section in range(lax.axis_size("species") - 1):
        carried = factor_chain * from_behind(carried, "species", 1) + own_part
    weighted = jnp.dot(
        gamma_yield[0],
        carried.reshape(bins, -1),
        precision=lax.Precision.HIGHEST,
        preferred_element_type=jnp.float32,
    )
    depth = carried.shape[3]
    emission = (
        jnp.sum(weighted.reshape(width, carried.shape[2], depth), axis=2) / (bins * depth)
    ).astype(jnp.bfloat16)
    columns = emission.reshape(-1)
    contribution = jnp.einsum(
        "c,lcb->lb", columns, sky_weight[0], preferred_element_type=jnp.float32
    )
    onehot = (sky_blocks[0][:, None] == jnp.arange(NB, dtype=jnp.int32)[None, :]).astype(
        jnp.float32
    )
    dense_map = jnp.dot(
        onehot.T, contribution, precision=lax.Precision.HIGHEST, preferred_element_type=jnp.float32
    )
    summed = lax.psum(dense_map, "species")
    sky = lax.psum_scatter(summed, "space", scatter_dimension=0, tiled=True)
    return (carried[None], sky)


def solution(mesh):
    placed = (
        P("species", None, "space", None, None),
        P("space", None, None),
        P("species", None),
        P("species", None, None),
        P("species", None),
        P("species", None),
        P("species", None),
        P("space", None, None, None),
        P("space", None),
    )
    return jax.shard_map(
        body,
        mesh=mesh,
        in_specs=placed,
        out_specs=(P("species", None, "space", None, None), P("space", None)),
        check_vma=False,
    )
```

profile of v0, /device:TPU:0, one launch (start us, length us, event | category | flops | bytes accessed | tf_op | source)
XLA Modules:
  0.0 190.8 jit_solution(6497044509966995586)
XLA Ops:
  7.3 1.4 fusion.25
  8.6 1.3 collective-permute-start
  9.9 3.1 %collective-permute-start.1 = (f32[32,1,32,128]{3,2,1,0:T(8,128)S(1)}, f32[32,1,32,128]{3,2,1,0:T(8,128)S(1)}, u32[]{:S(2)}, u32[]{:S(2)}) collective-permute-start(f32[32,1,32,128]{3,2,1,0:T(8,128)S(1)} %get-tuple-element.5), channel_id=1, source_target_pairs={{0,1},{1,2},{2,3},{3,4},{4,5},{5,6},{6,7},{8,9},{9,10},{10,11},{11... | collective-permute-start | bytes 1572872 | tf_op jit(solution)/shard_map/ppermute | solution.py:18
  13.0 1.5 collective-permute-done.1
  14.5 0.8 fusion
  15.4 1.3 collective-permute-start.2
  16.7 10.4 %collective-permute-start.3 = (f32[32,1,32,128]{3,2,1,0:T(8,128)S(1)}, f32[32,1,32,128]{3,2,1,0:T(8,128)S(1)}, u32[]{:S(2)}, u32[]{:S(2)}) collective-permute-start(f32[32,1,32,128]{3,2,1,0:T(8,128)S(1)} %get-tuple-element.3), channel_id=1, source_target_pairs={{0,1},{1,2},{2,3},{3,4},{4,5},{5,6},{6,7},{8,9},{9,10},{10,11},{11... | collective-permute-start | bytes 1572872 | tf_op jit(solution)/shard_map/ppermute | solution.py:18
  27.1 1.5 collective-permute-done.3
  28.6 0.8 fusion.1
  29.4 1.7 convolution_bitcast_fusion
  31.1 0.2 copy.16
  31.3 0.5 copy-done.5
  31.7 0.1 broadcast_multiply_fusion
  31.9 3.5 %collective-permute-start.4 = (f32[32,2,32,128]{3,2,1,0:T(8,128)S(1)}, f32[32,2,32,128]{3,2,1,0:T(8,128)S(1)}, u32[]{:S(2)}, u32[]{:S(2)}) collective-permute-start(f32[32,2,32,128]{3,2,1,0:T(8,128)S(1)} %broadcast_multiply_fusion), channel_id=1, source_target_pairs={{0,8},{8,16},{16,24},{1,9},{9,17},{17,25},{2,10},{10,18},{18,26},{... | collective-permute-start | bytes 3145736 | tf_op jit(solution)/shard_map/ppermute | solution.py:30
  35.4 18.0 %collective-permute-done.4 = f32[32,2,32,128]{3,2,1,0:T(8,128)S(1)} collective-permute-done((f32[32,2,32,128]{3,2,1,0:T(8,128)S(1)}, f32[32,2,32,128]{3,2,1,0:T(8,128)S(1)}, u32[]{:S(2)}, u32[]{:S(2)}) %collective-permute-start.4) | collective-permute-done | bytes 1048608 | tf_op jit(solution)/shard_map/ppermute | solution.py:30
  53.4 0.2 multiply_add_fusion.2
  53.6 4.5 %collective-permute-start.5 = (f32[32,2,32,128]{3,2,1,0:T(8,128)S(1)}, f32[32,2,32,128]{3,2,1,0:T(8,128)S(1)}, u32[]{:S(2)}, u32[]{:S(2)}) collective-permute-start(f32[32,2,32,128]{3,2,1,0:T(8,128)S(1)} %multiply_add_fusion.2), channel_id=1, source_target_pairs={{0,8},{8,16},{16,24},{1,9},{9,17},{17,25},{2,10},{10,18},{18,26},{... | collective-permute-start | bytes 3145736 | tf_op jit(solution)/shard_map/ppermute | solution.py:30
  58.1 19.1 %collective-permute-done.5 = f32[32,2,32,128]{3,2,1,0:T(8,128)S(1)} collective-permute-done((f32[32,2,32,128]{3,2,1,0:T(8,128)S(1)}, f32[32,2,32,128]{3,2,1,0:T(8,128)S(1)}, u32[]{:S(2)}, u32[]{:S(2)}) %collective-permute-start.5) | collective-permute-done | bytes 1048608 | tf_op jit(solution)/shard_map/ppermute | solution.py:30
  77.1 0.2 multiply_add_fusion.1
  77.3 4.5 %collective-permute-start.6 = (f32[32,2,32,128]{3,2,1,0:T(8,128)S(1)}, f32[32,2,32,128]{3,2,1,0:T(8,128)S(1)}, u32[]{:S(2)}, u32[]{:S(2)}) collective-permute-start(f32[32,2,32,128]{3,2,1,0:T(8,128)S(1)} %multiply_add_fusion.1), channel_id=1, source_target_pairs={{0,8},{8,16},{16,24},{1,9},{9,17},{17,25},{2,10},{10,18},{18,26},{... | collective-permute-start | bytes 3145736 | tf_op jit(solution)/shard_map/ppermute | solution.py:30
  81.8 20.1 %collective-permute-done.6 = f32[32,2,32,128]{3,2,1,0:T(8,128)S(1)} collective-permute-done((f32[32,2,32,128]{3,2,1,0:T(8,128)S(1)}, f32[32,2,32,128]{3,2,1,0:T(8,128)S(1)}, u32[]{:S(2)}, u32[]{:S(2)}) %collective-permute-start.6) | collective-permute-done | bytes 1048608 | tf_op jit(solution)/shard_map/ppermute | solution.py:30
  101.9 0.2 multiply_add_fusion
  102.1 0.6 copy.26
  102.7 0.3 copy-done.2
  103.1 0.2 copy.18
  103.3 0.5 copy-done.8
  103.7 1.2 fusion.16
  105.0 0.1 reduce_sum.9
  105.2 0.1 fusion.18
  105.3 1.1 fusion.21
  106.4 57.4 %reduce-scatter.2.cloned.1.call-done = f32[48,128]{1,0:T(8,128)} async-done(((f32[384,128]{1,0:T(8,128)}), f32[48,128]{1,0:T(8,128)}) %reduce-scatter.2.cloned.1.call-update) | async-done | bytes 24592 | tf_op jit(solution)/shard_map/reduce_scatter | solution.py:92
  163.8 20.2 %psum.8 = f32[48,128]{1,0:T(8,128)} all-reduce(f32[48,128]{1,0:T(8,128)} %reduce-scatter.2.cloned.1.call-done), channel_id=1, replica_groups=mesh['species'=4,'space'=8] {'species'}, use_global_device_ids=true, to_apply=%region_1.2 | all-reduce | flops 6144 | bytes 49152 | tf_op jit(solution)/shard_map/psum | solution.py:91
  (24 shorter events, 0.3 us)
Async XLA Ops:
  7.2 98.0 %copy-start = (bf16[1,8,64,128]{3,2,1,0:T(8,128)(2,1)S(1)}, bf16[1,8,64,128]{3,2,1,0:T(8,128)(2,1)}, u32[]{:S(2)}) copy-start(bf16[1,8,64,128]{3,2,1,0:T(8,128)(2,1)} %param.16) | copy-start | bytes 393220
  7.2 156.6 %reduce-scatter.2.cloned.1.call-start = ((), (), s32[]{:S(2)}) async-start(), calls=%async_computation.1 | async-start | bytes 221184 | tf_op jit(solution)/shard_map/reduce_scatter | solution.py:92
  7.2 7.3 %copy-start.1 = (f32[1,32,2,32,128]{4,3,2,1,0:T(8,128)S(1)}, f32[1,32,2,32,128]{4,3,2,1,0:T(8,128)}, u32[]{:S(2)}) copy-start(f32[1,32,2,32,128]{4,3,2,1,0:T(8,128)} %param.9) | copy-start | bytes 3145732
  7.2 7.3 %copy-start.3 = (f32[2,32,128]{2,1,0:T(8,128)S(1)}, f32[2,32,128]{2,1,0:T(8,128)}, u32[]{:S(2)}) copy-start(f32[2,32,128]{2,1,0:T(8,128)} %param.10) | copy-start | bytes 98308
  7.2 7.2 %copy-start.7 = (f32[1,32]{1,0:T(1,128)S(1)}, f32[1,32]{1,0:T(1,128)}, u32[]{:S(2)}) copy-start(f32[1,32]{1,0:T(1,128)} %param.11) | copy-start | bytes 388
  8.6 4.4 %collective-permute-start = (f32[32,1,32,128]{3,2,1,0:T(8,128)S(1)}, f32[32,1,32,128]{3,2,1,0:T(8,128)S(1)}, u32[]{:S(2)}, u32[]{:S(2)}) collective-permute-start(f32[32,1,32,128]{3,2,1,0:T(8,128)S(1)} %get-tuple-element.4), channel_id=1, source_target_pairs={{1,0},{2,1},{3,2},{4,3},{5,4},{6,5},{7,6},{9,8},{10,9},{11,10},{12... | collective-permute-start | bytes 1572872 | tf_op jit(solution)/shard_map/ppermute | solution.py:20
  9.9 4.6 %collective-permute-start.1 = (f32[32,1,32,128]{3,2,1,0:T(8,128)S(1)}, f32[32,1,32,128]{3,2,1,0:T(8,128)S(1)}, u32[]{:S(2)}, u32[]{:S(2)}) collective-permute-start(f32[32,1,32,128]{3,2,1,0:T(8,128)S(1)} %get-tuple-element.5), channel_id=1, source_target_pairs={{0,1},{1,2},{2,3},{3,4},{4,5},{5,6},{6,7},{8,9},{9,10},{10,11},{11... | collective-permute-start | bytes 1572872 | tf_op jit(solution)/shard_map/ppermute | solution.py:18
  15.4 11.7 %collective-permute-start.2 = (f32[32,1,32,128]{3,2,1,0:T(8,128)S(1)}, f32[32,1,32,128]{3,2,1,0:T(8,128)S(1)}, u32[]{:S(2)}, u32[]{:S(2)}) collective-permute-start(f32[32,1,32,128]{3,2,1,0:T(8,128)S(1)} %get-tuple-element.2), channel_id=1, source_target_pairs={{1,0},{2,1},{3,2},{4,3},{5,4},{6,5},{7,6},{9,8},{10,9},{11,10},{12... | collective-permute-start | bytes 1572872 | tf_op jit(solution)/shard_map/ppermute | solution.py:20
  16.7 12.7 %copy-start.4 = (f32[1,32,32]{2,1,0:T(8,128)S(1)}, f32[1,32,32]{2,1,0:T(8,128)}, u32[]{:S(2)}) copy-start(f32[1,32,32]{2,1,0:T(8,128)} %param.12) | copy-start | bytes 12292
  16.7 11.9 %collective-permute-start.3 = (f32[32,1,32,128]{3,2,1,0:T(8,128)S(1)}, f32[32,1,32,128]{3,2,1,0:T(8,128)S(1)}, u32[]{:S(2)}, u32[]{:S(2)}) collective-permute-start(f32[32,1,32,128]{3,2,1,0:T(8,128)S(1)} %get-tuple-element.3), channel_id=1, source_target_pairs={{0,1},{1,2},{2,3},{3,4},{4,5},{5,6},{6,7},{8,9},{9,10},{10,11},{11... | collective-permute-start | bytes 1572872 | tf_op jit(solution)/shard_map/ppermute | solution.py:18
  31.1 0.7 copy-start.5
  31.7 21.7 %copy-start.6 = (f32[1,32]{1,0:T(1,128)S(1)}, f32[1,32]{1,0:T(1,128)}, u32[]{:S(2)}) copy-start(f32[1,32]{1,0:T(1,128)} %param.13) | copy-start | bytes 388
  31.9 21.5 %collective-permute-start.4 = (f32[32,2,32,128]{3,2,1,0:T(8,128)S(1)}, f32[32,2,32,128]{3,2,1,0:T(8,128)S(1)}, u32[]{:S(2)}, u32[]{:S(2)}) collective-permute-start(f32[32,2,32,128]{3,2,1,0:T(8,128)S(1)} %broadcast_multiply_fusion), channel_id=1, source_target_pairs={{0,8},{8,16},{16,24},{1,9},{9,17},{17,25},{2,10},{10,18},{18,26},{... | collective-permute-start | bytes 3145736 | tf_op jit(solution)/shard_map/ppermute | solution.py:30
  53.6 23.5 %collective-permute-start.5 = (f32[32,2,32,128]{3,2,1,0:T(8,128)S(1)}, f32[32,2,32,128]{3,2,1,0:T(8,128)S(1)}, u32[]{:S(2)}, u32[]{:S(2)}) collective-permute-start(f32[32,2,32,128]{3,2,1,0:T(8,128)S(1)} %multiply_add_fusion.2), channel_id=1, source_target_pairs={{0,8},{8,16},{16,24},{1,9},{9,17},{17,25},{2,10},{10,18},{18,26},{... | collective-permute-start | bytes 3145736 | tf_op jit(solution)/shard_map/ppermute | solution.py:30
  77.3 24.6 %collective-permute-start.6 = (f32[32,2,32,128]{3,2,1,0:T(8,128)S(1)}, f32[32,2,32,128]{3,2,1,0:T(8,128)S(1)}, u32[]{:S(2)}, u32[]{:S(2)}) collective-permute-start(f32[32,2,32,128]{3,2,1,0:T(8,128)S(1)} %multiply_add_fusion.1), channel_id=1, source_target_pairs={{0,8},{8,16},{16,24},{1,9},{9,17},{17,25},{2,10},{10,18},{18,26},{... | collective-permute-start | bytes 3145736 | tf_op jit(solution)/shard_map/ppermute | solution.py:30
  102.1 1.0 copy-start.2
  103.1 0.7 copy-start.8
  103.3 2.0 %copy-start.9 = (s32[1,8]{1,0:T(1,128)S(1)}, s32[1,8]{1,0:T(1,128)}, u32[]{:S(2)}) copy-start(s32[1,8]{1,0:T(1,128)} %param.17) | copy-start | bytes 100
Sparse Core Ops, SparseCore 0:
  106.6 57.1 reduce-scatter.1
where the time goes:
time: 191 us
  waiting for transfers between devices  118 us (62%)
  starting transfers between devices  28.5 us (15%)
  blocking collectives  20.2 us (11%)
  between operations  14.3 us (7%)
  matrix products  4.16 us (2%)
  local copies, waits for them, and re-layouts  3.81 us (2%)
  other arithmetic  2.35 us (1%)
    reduce_scatter x1, waiting for transfers between devices, body(): sky = lax.psum_scatter(summed, 'space', scatter_dimension=0, tiled=True)  57.4 us
    ppermute x3, waiting for transfers between devices, from_behind(): return lax.ppermute(block, axis, route)  57.2 us
    psum x1, blocking collectives, body(): summed = lax.psum(dense_map, 'species')  20.2 us
    ppermute x2, starting transfers between devices, padded_2(): lax.ppermute(tail, axis, [(i, (i + 1) % count) for i in range(ends)])  13.5 us
    ppermute x3, starting transfers between devices, from_behind(): return lax.ppermute(block, axis, route)  12.5 us
  transfers between devices with their start and end apart: 8, of which 6 were waited for; matrix products, arithmetic and copies ran while one was open for 0% of the time, Pallas kernels for 0%

commit v1 on v0

--- a/solution.py
+++ b/solution.py
@@ -88,7 +88,7 @@
     dense_map = jnp.dot(
         onehot.T, contribution, precision=lax.Precision.HIGHEST, preferred_element_type=jnp.float32
     )
-    summed = lax.psum(dense_map, "species")
+    summed = jnp.sum(lax.all_gather(dense_map, "species"), axis=0)
     sky = lax.psum_scatter(summed, "space", scatter_dimension=0, tiled=True)
     return (carried[None], sky)
 

time: 191 us -> 189 us (0.990)
  waiting for transfers between devices: 118 us -> 116 us
    psum x1 -> x0, blocking collectives: 20.2 us -> none  [body(): summed = lax.psum(dense_map, 'species')]
    all_gather x0 -> x1, blocking collectives: none -> 19.2 us  [body(): summed = jnp.sum(lax.all_gather(dense_map, 'species'), axis=0)]
where the time goes in v1:
time: 189 us; the launch traced here: 188 us
  waiting for transfers between devices  116 us (61%)
  starting transfers between devices  28.5 us (15%)
  blocking collectives  19.2 us (10%)
  between operations  14.3 us (8%)
  local copies, waits for them, and re-layouts  3.81 us (2%)
  matrix products  3.47 us (2%)
  other arithmetic  3.07 us (2%)
    ppermute x3, waiting for transfers between devices, from_behind(): return lax.ppermute(block, axis, route)  57.2 us
    reduce_scatter x1, waiting for transfers between devices, body(): sky = lax.psum_scatter(summed, 'space', scatter_dimension=0, tiled=True)  55.8 us
    all_gather x1, blocking collectives, body(): summed = jnp.sum(lax.all_gather(dense_map, 'species'), axis=0)  19.2 us
    ppermute x2, starting transfers between devices, padded_2(): lax.ppermute(tail, axis, [(i, (i + 1) % count) for i in range(ends)])  13.5 us
    ppermute x3, starting transfers between devices, from_behind(): return lax.ppermute(block, axis, route)  12.5 us
  transfers between devices with their start and end apart: 8, of which 6 were waited for; matrix products, arithmetic and copies ran while one was open for 0% of the time, Pallas kernels for 0%

profile of v1, /device:TPU:0, one launch (start us, length us, event | category | flops | bytes accessed | tf_op | source)
XLA Modules:
  0.0 188.3 jit_solution(13211925934727204894)
XLA Ops:
  7.3 1.4 fusion.25
  8.6 1.3 collective-permute-start
  9.9 3.1 %collective-permute-start.1 = (f32[32,1,32,128]{3,2,1,0:T(8,128)S(1)}, f32[32,1,32,128]{3,2,1,0:T(8,128)S(1)}, u32[]{:S(2)}, u32[]{:S(2)}) collective-permute-start(f32[32,1,32,128]{3,2,1,0:T(8,128)S(1)} %get-tuple-element.5), channel_id=1, source_target_pairs={{0,1},{1,2},{2,3},{3,4},{4,5},{5,6},{6,7},{8,9},{9,10},{10,11},{11... | collective-permute-start | bytes 1572872 | tf_op jit(solution)/shard_map/ppermute | solution.py:18
  13.0 1.5 collective-permute-done.1
  14.5 0.8 fusion
  15.4 1.3 collective-permute-start.2
  16.7 10.4 %collective-permute-start.3 = (f32[32,1,32,128]{3,2,1,0:T(8,128)S(1)}, f32[32,1,32,128]{3,2,1,0:T(8,128)S(1)}, u32[]{:S(2)}, u32[]{:S(2)}) collective-permute-start(f32[32,1,32,128]{3,2,1,0:T(8,128)S(1)} %get-tuple-element.3), channel_id=1, source_target_pairs={{0,1},{1,2},{2,3},{3,4},{4,5},{5,6},{6,7},{8,9},{9,10},{10,11},{11... | collective-permute-start | bytes 1572872 | tf_op jit(solution)/shard_map/ppermute | solution.py:18
  27.1 1.5 collective-permute-done.3
  28.6 0.8 fusion.1
  29.4 1.7 convolution_bitcast_fusion
  31.1 0.2 copy.16
  31.3 0.5 copy-done.5
  31.7 0.1 broadcast_multiply_fusion
  31.9 3.5 %collective-permute-start.4 = (f32[32,2,32,128]{3,2,1,0:T(8,128)S(1)}, f32[32,2,32,128]{3,2,1,0:T(8,128)S(1)}, u32[]{:S(2)}, u32[]{:S(2)}) collective-permute-start(f32[32,2,32,128]{3,2,1,0:T(8,128)S(1)} %broadcast_multiply_fusion), channel_id=1, source_target_pairs={{0,8},{8,16},{16,24},{1,9},{9,17},{17,25},{2,10},{10,18},{18,26},{... | collective-permute-start | bytes 3145736 | tf_op jit(solution)/shard_map/ppermute | solution.py:30
  35.4 18.0 %collective-permute-done.4 = f32[32,2,32,128]{3,2,1,0:T(8,128)S(1)} collective-permute-done((f32[32,2,32,128]{3,2,1,0:T(8,128)S(1)}, f32[32,2,32,128]{3,2,1,0:T(8,128)S(1)}, u32[]{:S(2)}, u32[]{:S(2)}) %collective-permute-start.4) | collective-permute-done | bytes 1048608 | tf_op jit(solution)/shard_map/ppermute | solution.py:30
  53.4 0.2 multiply_add_fusion.2
  53.6 4.5 %collective-permute-start.5 = (f32[32,2,32,128]{3,2,1,0:T(8,128)S(1)}, f32[32,2,32,128]{3,2,1,0:T(8,128)S(1)}, u32[]{:S(2)}, u32[]{:S(2)}) collective-permute-start(f32[32,2,32,128]{3,2,1,0:T(8,128)S(1)} %multiply_add_fusion.2), channel_id=1, source_target_pairs={{0,8},{8,16},{16,24},{1,9},{9,17},{17,25},{2,10},{10,18},{18,26},{... | collective-permute-start | bytes 3145736 | tf_op jit(solution)/shard_map/ppermute | solution.py:30
  58.1 19.1 %collective-permute-done.5 = f32[32,2,32,128]{3,2,1,0:T(8,128)S(1)} collective-permute-done((f32[32,2,32,128]{3,2,1,0:T(8,128)S(1)}, f32[32,2,32,128]{3,2,1,0:T(8,128)S(1)}, u32[]{:S(2)}, u32[]{:S(2)}) %collective-permute-start.5) | collective-permute-done | bytes 1048608 | tf_op jit(solution)/shard_map/ppermute | solution.py:30
  77.1 0.2 multiply_add_fusion.1
  77.3 4.5 %collective-permute-start.6 = (f32[32,2,32,128]{3,2,1,0:T(8,128)S(1)}, f32[32,2,32,128]{3,2,1,0:T(8,128)S(1)}, u32[]{:S(2)}, u32[]{:S(2)}) collective-permute-start(f32[32,2,32,128]{3,2,1,0:T(8,128)S(1)} %multiply_add_fusion.1), channel_id=1, source_target_pairs={{0,8},{8,16},{16,24},{1,9},{9,17},{17,25},{2,10},{10,18},{18,26},{... | collective-permute-start | bytes 3145736 | tf_op jit(solution)/shard_map/ppermute | solution.py:30
  81.8 20.1 %collective-permute-done.6 = f32[32,2,32,128]{3,2,1,0:T(8,128)S(1)} collective-permute-done((f32[32,2,32,128]{3,2,1,0:T(8,128)S(1)}, f32[32,2,32,128]{3,2,1,0:T(8,128)S(1)}, u32[]{:S(2)}, u32[]{:S(2)}) %collective-permute-start.6) | collective-permute-done | bytes 1048608 | tf_op jit(solution)/shard_map/ppermute | solution.py:30
  101.9 0.2 multiply_add_fusion
  102.1 0.6 copy.26
  102.7 0.3 copy-done.2
  103.1 0.2 copy.18
  103.3 0.5 copy-done.8
  103.7 1.2 fusion.16
  105.2 0.1 fusion.18
  105.3 0.4 fusion.21
  105.7 19.2 %all-gather = f32[1536,128]{1,0:T(8,128)S(1)} all-gather(f32[384,128]{1,0:T(8,128)S(1)} %fusion.21), channel_id=2, replica_groups=mesh['species'=4,'space'=8] {'species'}, dimensions={0}, use_global_device_ids=true | all-gather | bytes 983040 | tf_op jit(solution)/shard_map/all_gather | solution.py:91
  124.9 0.7 reduce_sum.19
  125.7 55.8 %reduce-scatter.2.cloned.1.call-done = f32[48,128]{1,0:T(8,128)} async-done(((f32[384,128]{1,0:T(8,128)}), f32[48,128]{1,0:T(8,128)}) %reduce-scatter.2.cloned.1.call-update) | async-done | bytes 24592 | tf_op jit(solution)/shard_map/reduce_scatter | solution.py:92
  (25 shorter events, 0.4 us)
Async XLA Ops:
  7.2 98.0 %copy-start = (bf16[1,8,64,128]{3,2,1,0:T(8,128)(2,1)S(1)}, bf16[1,8,64,128]{3,2,1,0:T(8,128)(2,1)}, u32[]{:S(2)}) copy-start(bf16[1,8,64,128]{3,2,1,0:T(8,128)(2,1)} %param.16) | copy-start | bytes 393220
  7.2 174.3 %reduce-scatter.2.cloned.1.call-start = ((), (), s32[]{:S(2)}) async-start(), calls=%async_computation.1 | async-start | bytes 221184 | tf_op jit(solution)/shard_map/reduce_scatter | solution.py:92
  7.2 7.3 %copy-start.1 = (f32[1,32,2,32,128]{4,3,2,1,0:T(8,128)S(1)}, f32[1,32,2,32,128]{4,3,2,1,0:T(8,128)}, u32[]{:S(2)}) copy-start(f32[1,32,2,32,128]{4,3,2,1,0:T(8,128)} %param.9) | copy-start | bytes 3145732
  7.2 7.3 %copy-start.3 = (f32[2,32,128]{2,1,0:T(8,128)S(1)}, f32[2,32,128]{2,1,0:T(8,128)}, u32[]{:S(2)}) copy-start(f32[2,32,128]{2,1,0:T(8,128)} %param.10) | copy-start | bytes 98308
  7.2 7.2 %copy-start.7 = (f32[1,32]{1,0:T(1,128)S(1)}, f32[1,32]{1,0:T(1,128)}, u32[]{:S(2)}) copy-start(f32[1,32]{1,0:T(1,128)} %param.11) | copy-start | bytes 388
  8.6 4.4 %collective-permute-start = (f32[32,1,32,128]{3,2,1,0:T(8,128)S(1)}, f32[32,1,32,128]{3,2,1,0:T(8,128)S(1)}, u32[]{:S(2)}, u32[]{:S(2)}) collective-permute-start(f32[32,1,32,128]{3,2,1,0:T(8,128)S(1)} %get-tuple-element.4), channel_id=1, source_target_pairs={{1,0},{2,1},{3,2},{4,3},{5,4},{6,5},{7,6},{9,8},{10,9},{11,10},{12... | collective-permute-start | bytes 1572872 | tf_op jit(solution)/shard_map/ppermute | solution.py:20
  9.9 4.6 %collective-permute-start.1 = (f32[32,1,32,128]{3,2,1,0:T(8,128)S(1)}, f32[32,1,32,128]{3,2,1,0:T(8,128)S(1)}, u32[]{:S(2)}, u32[]{:S(2)}) collective-permute-start(f32[32,1,32,128]{3,2,1,0:T(8,128)S(1)} %get-tuple-element.5), channel_id=1, source_target_pairs={{0,1},{1,2},{2,3},{3,4},{4,5},{5,6},{6,7},{8,9},{9,10},{10,11},{11... | collective-permute-start | bytes 1572872 | tf_op jit(solution)/shard_map/ppermute | solution.py:18
  15.4 11.7 %collective-permute-start.2 = (f32[32,1,32,128]{3,2,1,0:T(8,128)S(1)}, f32[32,1,32,128]{3,2,1,0:T(8,128)S(1)}, u32[]{:S(2)}, u32[]{:S(2)}) collective-permute-start(f32[32,1,32,128]{3,2,1,0:T(8,128)S(1)} %get-tuple-element.2), channel_id=1, source_target_pairs={{1,0},{2,1},{3,2},{4,3},{5,4},{6,5},{7,6},{9,8},{10,9},{11,10},{12... | collective-permute-start | bytes 1572872 | tf_op jit(solution)/shard_map/ppermute | solution.py:20
  16.7 12.7 %copy-start.4 = (f32[1,32,32]{2,1,0:T(8,128)S(1)}, f32[1,32,32]{2,1,0:T(8,128)}, u32[]{:S(2)}) copy-start(f32[1,32,32]{2,1,0:T(8,128)} %param.12) | copy-start | bytes 12292
  16.7 11.9 %collective-permute-start.3 = (f32[32,1,32,128]{3,2,1,0:T(8,128)S(1)}, f32[32,1,32,128]{3,2,1,0:T(8,128)S(1)}, u32[]{:S(2)}, u32[]{:S(2)}) collective-permute-start(f32[32,1,32,128]{3,2,1,0:T(8,128)S(1)} %get-tuple-element.3), channel_id=1, source_target_pairs={{0,1},{1,2},{2,3},{3,4},{4,5},{5,6},{6,7},{8,9},{9,10},{10,11},{11... | collective-permute-start | bytes 1572872 | tf_op jit(solution)/shard_map/ppermute | solution.py:18
  31.1 0.7 copy-start.5
  31.7 21.7 %copy-start.6 = (f32[1,32]{1,0:T(1,128)S(1)}, f32[1,32]{1,0:T(1,128)}, u32[]{:S(2)}) copy-start(f32[1,32]{1,0:T(1,128)} %param.13) | copy-start | bytes 388
  31.9 21.5 %collective-permute-start.4 = (f32[32,2,32,128]{3,2,1,0:T(8,128)S(1)}, f32[32,2,32,128]{3,2,1,0:T(8,128)S(1)}, u32[]{:S(2)}, u32[]{:S(2)}) collective-permute-start(f32[32,2,32,128]{3,2,1,0:T(8,128)S(1)} %broadcast_multiply_fusion), channel_id=1, source_target_pairs={{0,8},{8,16},{16,24},{1,9},{9,17},{17,25},{2,10},{10,18},{18,26},{... | collective-permute-start | bytes 3145736 | tf_op jit(solution)/shard_map/ppermute | solution.py:30
  53.6 23.5 %collective-permute-start.5 = (f32[32,2,32,128]{3,2,1,0:T(8,128)S(1)}, f32[32,2,32,128]{3,2,1,0:T(8,128)S(1)}, u32[]{:S(2)}, u32[]{:S(2)}) collective-permute-start(f32[32,2,32,128]{3,2,1,0:T(8,128)S(1)} %multiply_add_fusion.2), channel_id=1, source_target_pairs={{0,8},{8,16},{16,24},{1,9},{9,17},{17,25},{2,10},{10,18},{18,26},{... | collective-permute-start | bytes 3145736 | tf_op jit(solution)/shard_map/ppermute | solution.py:30
  77.3 24.6 %collective-permute-start.6 = (f32[32,2,32,128]{3,2,1,0:T(8,128)S(1)}, f32[32,2,32,128]{3,2,1,0:T(8,128)S(1)}, u32[]{:S(2)}, u32[]{:S(2)}) collective-permute-start(f32[32,2,32,128]{3,2,1,0:T(8,128)S(1)} %multiply_add_fusion.1), channel_id=1, source_target_pairs={{0,8},{8,16},{16,24},{1,9},{9,17},{17,25},{2,10},{10,18},{18,26},{... | collective-permute-start | bytes 3145736 | tf_op jit(solution)/shard_map/ppermute | solution.py:30
  102.1 1.0 copy-start.2
  103.1 0.7 copy-start.8
  103.3 2.0 %copy-start.9 = (s32[1,8]{1,0:T(1,128)S(1)}, s32[1,8]{1,0:T(1,128)}, u32[]{:S(2)}) copy-start(s32[1,8]{1,0:T(1,128)} %param.17) | copy-start | bytes 100
Sparse Core Ops, SparseCore 0:
  125.8 55.6 reduce-scatter.1
